TPU v7x, 256 devices: a whole 4x4x8 slice. The times are simulated.
256 devices in a mesh: guide: 2 (over x_hi), req: 128 (over x_lo, y, z, core).
Axes of the slice: x: 4 (x_hi: 2, x_lo: 2; x = x_hi * 2 + x_lo), y: 4, z: 8, core: 2. Of those that a mesh axis runs over, the one named last changes fastest.
Arguments:
- hidden_in: bfloat16 [2, 3072, 2048], P('guide', 'req'), may hold values from -24 to 24
- attn_gain: float32 [2048], replicated, may hold values from 0.25 to 1.75
- w_qkv: bfloat16 [2048, 1920], P('guide'), may hold values from -0.125 to 0.125
- w_out: bfloat16 [1280, 2048], P('guide'), may hold values from -0.3125 to 0.3125
- final_gain: float32 [2048], replicated, may hold values from 0.25 to 1.75
- w_vocab: bfloat16 [2048, 32000], P(None, 'req'), may hold values from -0.125 to 0.125
- kv_pool: bfloat16 [2, 5888, 64, 640], P('guide', 'req'), may hold values from -1400 to 1400
- cache_len: int32 [2, 3072], P('guide'), may hold values from 1 to 512, as said below
- page_table: int32 [2, 3072, 8], P('guide'), may hold values from 0 to 45, as said below
- migrations: int32 [2, 128, 3], P('guide'), may hold values from 0 to 3071, as said below
Outputs:
- guided: float32 [3072, 32000], P('guide', 'req')
Inputs may be any that keep to these rules, and one draw needn't show every extreme that they name: `cache_len`: cached tokens of a request of group 0 number at most 512, of group 1 at most 256; both bounds are reached in each group. `page_table`: row i lists request i's pages in order as numbers within the pool of its owner (old owner if listed, else req index i // 24); entries past its last page are 0; pages of different requests on one device differ. `migrations`: 128 rows per group, distinct requests; the new owner is request // 24; the old owner differs from it by 1 to 2 modulo 128; at most one row per pair of owners; a listed request has at most 2 pages; in each group some new owner receives, from each of its 4 nearest old owners, a request of 2 pages.
All inputs are finite; a program needn't handle non-finite values.
Results may differ from a plain program's by a relative error of at most 0.011.
The roundings to bfloat16 on the way count: a program that leaves them out, or rounds other values in their place, can miss the bound.
Values may be sent and summed in bfloat16 or wider, within the bound.
No kernel may reach another device: no remote copies, remote signals or barrier semaphores. Data moves between devices by JAX's collectives and lax.ppermute only.
A program may use at most 128 MiB of HBM per device.

v0:
```python
import math
import jax
import jax.numpy as jnp
from jax import lax
from jax.sharding import PartitionSpec as P

QH = 20
KVH = 5
HD = 64
MAXP = 8
MIGP = 2
HOP = 2
epsilon = 1e-06
guidance = 3.0


def from_partner(block, axis, bit):
    count = lax.axis_size(axis)
    route = []
    for low in range(count):
        high = low | 1 << bit
        if high != low and high < count:
            route += [(low, high), (high, low)]
    return lax.ppermute(block, axis, route)


def shifted(value, axis, steps):
    count = lax.axis_size(axis)
    pairs = [(source, (source + steps) % count) for source in range(count)]
    return lax.ppermute(value, axis, pairs)


def rms_scale(values, gain):
    return values * lax.rsqrt(jnp.mean(values * values, axis=-1, keepdims=True) + epsilon) * gain


def masked_scores(queries, page_rows, lengths):
    count = page_rows.shape[0]
    span = page_rows.shape[1]
    half_width = page_rows.shape[2] // 2
    key_rows = page_rows[:, :, :half_width].reshape(count, span, KVH, HD)
    value_rows = page_rows[:, :, half_width:].reshape(count, span, KVH, HD)
    scores = jnp.einsum(
        "rkgd,rskd->rkgs", queries, key_rows, preferred_element_type=jnp.float32
    ) * (1.0 / math.sqrt(HD))
    living = jnp.arange(span, dtype=jnp.int32)[None, :] < lengths[:, None]
    scores = jnp.where(living[:, None, None, :], scores, -jnp.inf)
    return (scores, value_rows)


def attend_all(queries, page_rows, lengths, own_score, value_new):
    scores, value_rows = masked_scores(queries, page_rows, lengths)
    highest = jnp.maximum(jnp.max(scores, axis=-1), own_score)
    weights = jnp.exp(scores - highest[..., None])
    own_weight = jnp.exp(own_score - highest)
    denominator = jnp.sum(weights, axis=-1) + own_weight
    weighted = jnp.einsum(
        "rkgs,rskd->rkgd",
        weights.astype(jnp.bfloat16),
        value_rows,
        preferred_element_type=jnp.float32,
    )
    own_rounded = own_weight.astype(jnp.bfloat16).astype(jnp.float32)
    weighted = weighted + own_rounded[..., None] * value_new.astype(jnp.float32)[:, :, None, :]
    return (highest, denominator, weighted)


def gather_pages(pool, tables):
    picked = pool[tables]
    return picked.reshape(tables.shape[0], tables.shape[1] * pool.shape[1], pool.shape[2])


def body(
    hidden_in,
    attn_gain,
    w_qkv,
    w_out,
    final_gain,
    w_vocab,
    kv_pool,
    cache_len,
    page_table,
    migrations,
):
    device = lax.axis_index("req")
    devices = lax.axis_size("req")
    side = lax.axis_index("guide")
    local_rows = hidden_in.shape[1]
    group = QH // KVH
    query_width = QH * HD
    key_width = KVH * HD
    scaling = 1.0 / math.sqrt(HD)
    slots = 2 * HOP
    offsets = [number - HOP if number < HOP else number - HOP + 1 for number in range(slots)]
    states_in = hidden_in[0].astype(jnp.float32)
    normed = rms_scale(states_in, attn_gain).astype(jnp.bfloat16)
    partner_normed = from_partner(normed, "guide", 0)
    both_normed = jnp.where(
        side == 0, jnp.stack([normed, partner_normed]), jnp.stack([partner_normed, normed])
    )
    inner_half = w_qkv.shape[0]
    normed_part = lax.dynamic_slice_in_dim(both_normed, side * inner_half, inner_half, 2)
    selected = normed_part
    joined = lax.psum_scatter(
        jnp.einsum("grd,df->grf", selected, w_qkv, preferred_element_type=jnp.float32),
        "guide",
        scatter_dimension=0,
        tiled=True,
    )[0].astype(jnp.bfloat16)
    queries = joined[:, :query_width].reshape(local_rows, KVH, group, HD)
    new_keys = joined[:, query_width : query_width + key_width].reshape(local_rows, KVH, HD)
    new_values = joined[:, query_width + key_width :].reshape(local_rows, KVH, HD)
    own_score = (
        jnp.einsum("rkgd,rkd->rkg", queries, new_keys, preferred_element_type=jnp.float32) * scaling
    )
    tables = page_table[0]
    lengths_all = cache_len[0]
    listing = migrations[0]
    pool = kv_pool[0]
    pool_pages = pool.shape[0]
    first_row = device * local_rows
    own_table = lax.dynamic_slice_in_dim(tables, first_row, local_rows, 0)
    own_lengths = lax.dynamic_slice_in_dim(lengths_all, first_row, local_rows, 0)
    global_ids = first_row + jnp.arange(local_rows, dtype=jnp.int32)
    matches = listing[None, :, 0] == global_ids[:, None]
    is_moved = jnp.any(matches, axis=1)
    old_owner = jnp.sum(jnp.where(matches, listing[None, :, 1], 0), axis=1)
    distance = jnp.remainder(device - old_owner, devices)
    slot_of = jnp.where(distance <= HOP, HOP + distance - 1, HOP - (devices - distance))
    arrivals = []
    for number in range(slots):
        offset = offsets[number]
        holding = (listing[:, 1] == device) & (
            listing[:, 2] == jnp.remainder(device + offset, devices)
        )
        held_request = listing[jnp.argmax(holding), 0]
        pages_sent = pool[tables[held_request, :MIGP]]
        arrivals.append(shifted(pages_sent, "req", offset))
    extended = jnp.concatenate([pool] + arrivals, axis=0)
    page_column = jnp.minimum(jnp.arange(MAXP, dtype=jnp.int32), MIGP - 1)
    moved_pages = pool_pages + slot_of[:, None] * MIGP + page_column[None, :]
    used_table = jnp.where(is_moved[:, None], moved_pages, own_table)
    tops, sums, accs = attend_all(
        queries, gather_pages(extended, used_table), own_lengths, own_score, new_values
    )
    attended = (accs / sums[..., None]).reshape(local_rows, query_width).astype(jnp.bfloat16)
    partner_attended = from_partner(attended, "guide", 0)
    both_attended = jnp.where(
        side == 0, jnp.stack([attended, partner_attended]), jnp.stack([partner_attended, attended])
    )
    head_half = w_out.shape[0]
    attended_part = lax.dynamic_slice_in_dim(both_attended, side * head_half, head_half, 2)
    selected = attended_part
    state_after = (
        states_in
        + lax.psum_scatter(
            jnp.einsum("grc,cd->grd", selected, w_out, preferred_element_type=jnp.float32).astype(
                jnp.bfloat16
            ),
            "guide",
            scatter_dimension=0,
            tiled=True,
        ).astype(jnp.float32)[0]
    )
    final = rms_scale(state_after, final_gain).astype(jnp.bfloat16)
    logits = jnp.dot(
        lax.all_gather(final, "req", axis=0, tiled=True),
        w_vocab,
        preferred_element_type=jnp.float32,
    )
    halves = logits.reshape(2, logits.shape[0] // 2, logits.shape[1])
    paired = lax.all_to_all(
        halves.astype(jnp.bfloat16), "guide", split_axis=0, concat_axis=0, tiled=True
    ).astype(halves.dtype)
    return paired[1] + guidance * (paired[0] - paired[1])


def solution(mesh):
    in_specs = (
        P("guide", "req", None),
        P(),
        P("guide", None),
        P("guide", None),
        P(),
        P(None, "req"),
        P("guide", "req", None, None),
        P("guide", None),
        P("guide", None, None),
        P("guide", None, None),
    )
    out_specs = P("guide", "req")
    return jax.shard_map(body, mesh=mesh, in_specs=in_specs, out_specs=out_specs, check_vma=False)
```

profile of v0, /device:TPU:32, one launch (start us, length us, event | category | flops | bytes accessed | tf_op | source)
XLA Modules:
  0.0 425.6 jit_solution(11976493014555277146)
XLA Ops:
  17.8 1.5 constant_dynamic-slice_fusion.8
  26.8 1.0 fusion.53
  27.9 2.6 gather_fusion
  30.5 1.9 collective-permute-start.1
  32.4 2.7 gather_fusion.1
  35.1 6.8 %collective-permute-start.2 = (bf16[2,64,640]{2,1,0:T(8,128)(2,1)S(1)}, bf16[2,64,640]{2,1,0:T(8,128)(2,1)S(1)}, u32[]{:S(2)}, u32[]{:S(2)}) collective-permute-start(bf16[2,64,640]{2,1,0:T(8,128)(2,1)S(1)} %gather_fusion.1), channel_id=1, source_target_pairs={{0,127},{1,0},{2,1},{3,2},{4,3},{5,4},{6,5},{7,6},{8,7},{9,8},{10,... | collective-permute-start | bytes 491528 | tf_op jit(solution)/shard_map/ppermute | solution.py:30
  41.9 3.3 gather_fusion.2
  45.2 3.3 gather_fusion.3
  48.5 1.0 fusion.20
  49.5 1.6 fusion.22
  51.1 2.7 collective-permute-start
  53.9 4.2 constant_dynamic-update-slice_fusion.4
  60.4 3.7 fusion
  65.8 1.6 constant_dynamic-update-slice_fusion.1
  67.4 1.6 constant_dynamic-update-slice_fusion
  69.0 11.3 %gather_fusion.4 = bf16[192,64,640]{2,1,0:T(8,128)(2,1)} fusion(bf16[54,64,640]{2,1,0:T(8,128)(2,1)} %constant_dynamic-update-slice_fusion, s32[1024]{0:T(1024)S(1)} %pad_clamp_fusion), kind=kCustom, calls=%fused_computation.4 | custom fusion | bytes 31458048 | tf_op jit(solution)/shard_map/gather | solution.py:69
  80.3 16.9 %fusion.64 = (bf16[24,512,320]{2,1,0:T(8,128)(2,1)}, bf16[24,512,320]{2,1,0:T(8,128)(2,1)}) fusion(bf16[24,512,640]{2,1,0:T(8,128)(2,1)} %bitcast.139), kind=kLoop, calls=%fused_computation.128 | loop fusion | bytes 31457280 | tf_op jit(solution)/shard_map/slice | solution.py:41
  97.2 11.6 %copy.27 = bf16[24,512,320]{1,2,0:T(8,128)(2,1)} copy(bf16[24,512,320]{2,1,0:T(8,128)(2,1)} %get-tuple-element.17) | data formatting | bytes 15728640
  108.7 11.5 %copy.28 = bf16[24,512,320]{1,2,0:T(8,128)(2,1)} copy(bf16[24,512,320]{2,1,0:T(8,128)(2,1)} %get-tuple-element.18) | data formatting | bytes 15728640
  120.2 0.9 convert_bitcast_fusion.1
  121.8 4.5 %fusion.65 = (f32[24,5,4]{2,1,0:T(8,128)S(1)}, f32[24,5,4,512]{3,2,1,0:T(4,128)S(1)}) fusion(bf16[24,5,4,64]{3,2,1,0:T(4,128)(2,1)S(1)} %reshape.351, bf16[24,512,5,64]{1,3,2,0:T(8,128)(2,1)} %bitcast.140, pred[24,512]{1,0:T(8,128)(4,1)S(1)} %iota_compare_fusion), kind=kOutput, calls=%fused_computation.129 | convolution fusion | flops 32194080 | bytes 8923008 | tf_op jit(solution)/shard_map/rkgd,rskd->rkgs/dot_general | solution.py:43
  126.3 0.9 copy-done.1
  127.9 5.8 %fusion.12 = bf16[24,5,4,64]{3,2,1,0:T(4,128)(2,1)S(1)} fusion(bf16[24,512,5,64]{1,3,2,0:T(8,128)(2,1)} %bitcast.141, f32[24,5,4,512]{3,2,1,0:T(4,128)} %copy-done.1, f32[24,5,4]{2,1,0:T(8,128)S(1)} %fusion.31, f32[24,5,4]{2,1,0:T(8,128)S(1)} %get-tuple-element.20, f32[24,5,64]{2,1,0:T(8,128)S(1)} %reshape.357, f32[24,5,4]{2,1,0:T(8,128)S(1)} %get-tuple-element.19), kind=kOutput, calls=%fused_computation.20 | convolution fusion | flops 32071680 | bytes 8945280 | tf_op jit(solution)/shard_map/rkgs,rskd->rkgd/dot_general | solution.py:57
  134.8 4.9 %collective-permute-done.5 = bf16[24,1280]{1,0:T(8,128)(2,1)S(1)} collective-permute-done((bf16[24,1280]{1,0:T(8,128)(2,1)S(1)}, bf16[24,1280]{1,0:T(8,128)(2,1)S(1)}, u32[]{:S(2)}, u32[]{:S(2)}) %collective-permute-start.5) | collective-permute-done | bytes 61472 | tf_op jit(solution)/shard_map/ppermute | solution.py:24
  139.7 1.2 fusion.4
  141.2 15.0 %reduce-scatter.5.cloned.1.call-done = bf16[1,24,2048]{2,1,0:T(8,128)(2,1)} async-done(((bf16[2,24,2048]{2,1,0:T(8,128)(2,1)}), bf16[1,24,2048]{2,1,0:T(8,128)(2,1)}) %reduce-scatter.5.cloned.1.call-update) | async-done | bytes 98320 | tf_op jit(solution)/shard_map/reduce_scatter | solution.py:156
  156.2 1.0 multiply_reduce_fusion
  157.3 1.6 multiply_convert_fusion
  158.9 225.8 %all-gather.2.cloned.1.call-done = bf16[3072,2048]{1,0:T(8,128)(2,1)} async-done(((bf16[24,2048]{1,0:T(8,128)(2,1)}), bf16[3072,2048]{1,0:T(8,128)(2,1)}) %all-gather.2.cloned.1.call-update) | async-done | bytes 12582928 | tf_op jit(solution)/shard_map/all_gather | solution.py:167
  384.7 8.2 %convolution_convert_fusion = bf16[3072,250]{1,0:T(8,128)(2,1)S(1)} fusion(bf16[3072,2048]{1,0:T(8,128)(2,1)} %all-gather.2.cloned.1.call-done, bf16[2048,250]{1,0:T(8,128)(2,1)} %param.15), kind=kOutput, calls=%fused_computation.7 | convolution fusion | flops 3146496000 | bytes 15142912 | tf_op jit(solution)/shard_map/dot_general | solution.py:166
  392.9 24.5 %all_to_all.5 = bf16[2,1536,250]{2,1,0:T(8,128)(2,1)S(1)} all-to-all(bf16[2,1536,250]{2,1,0:T(8,128)(2,1)S(1)} %bitcast.146), channel_id=1, replica_groups=mesh['guide'=2,'req'=128] {'guide'}, dimensions={0} | all-to-all | bytes 3072000 | tf_op jit(solution)/shard_map/all_to_all | solution.py:172
  417.7 1.3 fusion.9
  (64 shorter events, 10.5 us)
Async XLA Ops:
  6.5 133.2 %copy-start = (bf16[640,2048]{1,0:T(8,128)(2,1)S(1)}, bf16[640,2048]{1,0:T(8,128)(2,1)}, u32[]{:S(2)}) copy-start(bf16[640,2048]{1,0:T(8,128)(2,1)} %param.13) | copy-start | bytes 7864324
  6.5 113.7 %reduce-scatter.7.cloned.1.call-start = ((), (), s32[]{:S(2)}) async-start(), calls=%async_computation.5 | async-start | bytes 552960
  30.5 33.9 %collective-permute-start.1 = (bf16[2,64,640]{2,1,0:T(8,128)(2,1)S(1)}, bf16[2,64,640]{2,1,0:T(8,128)(2,1)S(1)}, u32[]{:S(2)}, u32[]{:S(2)}) collective-permute-start(bf16[2,64,640]{2,1,0:T(8,128)(2,1)S(1)} %gather_fusion), channel_id=1, source_target_pairs={{0,126},{1,127},{2,0},{3,1},{4,2},{5,3},{6,4},{7,5},{8,6},{9,7},{1... | collective-permute-start | bytes 491528 | tf_op jit(solution)/shard_map/ppermute | solution.py:30
  32.4 25.7 %copy-start.2 = (bf16[1,24,2048]{2,1,0:T(8,128)(2,1)S(1)}, bf16[1,24,2048]{2,1,0:T(8,128)(2,1)}, u32[]{:S(2)}) copy-start(bf16[1,24,2048]{2,1,0:T(8,128)(2,1)} %param.10) | copy-start | bytes 294916
  32.4 25.7 %copy-start.3 = (f32[2048]{0:T(1024)S(1)}, f32[2048]{0:T(1024)}, u32[]{:S(2)}) copy-start(f32[2048]{0:T(1024)} %param.11) | copy-start | bytes 24580
  35.1 30.0 %collective-permute-start.2 = (bf16[2,64,640]{2,1,0:T(8,128)(2,1)S(1)}, bf16[2,64,640]{2,1,0:T(8,128)(2,1)S(1)}, u32[]{:S(2)}, u32[]{:S(2)}) collective-permute-start(bf16[2,64,640]{2,1,0:T(8,128)(2,1)S(1)} %gather_fusion.1), channel_id=1, source_target_pairs={{0,127},{1,0},{2,1},{3,2},{4,3},{5,4},{6,5},{7,6},{8,7},{9,8},{10,... | collective-permute-start | bytes 491528 | tf_op jit(solution)/shard_map/ppermute | solution.py:30
  45.2 20.6 %collective-permute-start.3 = (bf16[2,64,640]{2,1,0:T(8,128)(2,1)}, bf16[2,64,640]{2,1,0:T(8,128)(2,1)}, u32[]{:S(2)}, u32[]{:S(2)}) collective-permute-start(bf16[2,64,640]{2,1,0:T(8,128)(2,1)} %gather_fusion.2), channel_id=1, source_target_pairs={{0,1},{1,2},{2,3},{3,4},{4,5},{5,6},{6,7},{7,8},{8,9},{9,10},{10,1... | collective-permute-start | bytes 491528 | tf_op jit(solution)/shard_map/ppermute | solution.py:30
  48.5 18.9 %collective-permute-start.4 = (bf16[2,64,640]{2,1,0:T(8,128)(2,1)}, bf16[2,64,640]{2,1,0:T(8,128)(2,1)}, u32[]{:S(2)}, u32[]{:S(2)}) collective-permute-start(bf16[2,64,640]{2,1,0:T(8,128)(2,1)} %gather_fusion.3), channel_id=1, source_target_pairs={{0,2},{1,3},{2,4},{3,5},{4,6},{5,7},{6,8},{7,9},{8,10},{9,11},{10,... | collective-permute-start | bytes 491528 | tf_op jit(solution)/shard_map/ppermute | solution.py:30
  51.1 9.3 %collective-permute-start = (bf16[24,2048]{1,0:T(8,128)(2,1)}, bf16[24,2048]{1,0:T(8,128)(2,1)}, u32[]{:S(2)}, u32[]{:S(2)}) collective-permute-start(bf16[24,2048]{1,0:T(8,128)(2,1)} %fusion.22), channel_id=1, source_target_pairs={{0,128},{128,0},{1,129},{129,1},{2,130},{130,2},{3,131},{131,3},{4... | collective-permute-start | bytes 294920 | tf_op jit(solution)/shard_map/ppermute | solution.py:24
  64.1 92.1 %reduce-scatter.5.cloned.1.call-start = ((), (), s32[]{:S(2)}) async-start(), calls=%async_computation.3 | async-start | bytes 294912 | tf_op jit(solution)/shard_map/reduce_scatter | solution.py:156
  126.2 0.9 copy-start.1
  133.7 23.5 %copy-start.4 = (f32[2048]{0:T(1024)S(1)}, f32[2048]{0:T(1024)}, u32[]{:S(2)}) copy-start(f32[2048]{0:T(1024)} %param.14) | copy-start | bytes 24580
  133.9 5.8 %collective-permute-start.5 = (bf16[24,1280]{1,0:T(8,128)(2,1)S(1)}, bf16[24,1280]{1,0:T(8,128)(2,1)S(1)}, u32[]{:S(2)}, u32[]{:S(2)}) collective-permute-start(bf16[24,1280]{1,0:T(8,128)(2,1)S(1)} %convert_element_type.86), channel_id=1, source_target_pairs={{0,128},{128,0},{1,129},{129,1},{2,130},{130,2},{3,131},{131,3},{4... | collective-permute-start | bytes 184328 | tf_op jit(solution)/shard_map/ppermute | solution.py:24
  141.0 243.7 %all-gather.2.cloned.1.call-start = ((), (), s32[]{:S(2)}) async-start(), calls=%async_computation.4 | async-start | bytes 12681216 | tf_op jit(solution)/shard_map/all_gather | solution.py:167
Sparse Core Ops, SparseCore 0:
  64.3 17.4 reduce-scatter.6
  141.1 15.0 reduce-scatter.4
  159.0 225.6 all-gather.1
where the time goes:
time: 427 us; the launch traced here: 426 us
  waiting for transfers between devices  246 us (58%)
  local copies, waits for them, and re-layouts  77.8 us (18%)
  between operations  28.5 us (7%)
  blocking collectives  24.5 us (6%)
  matrix products  23.7 us (6%)
  other arithmetic  12.8 us (3%)
  starting transfers between devices  12.6 us (3%)
    all_gather x1, waiting for transfers between devices, body(): lax.all_gather(final, 'req', axis=0, tiled=True)  226 us
    unnamed x17, local copies, waits for them, and re-layouts  32.1 us
    all_to_all x1, blocking collectives, body(): lax.all_to_all(halves.astype(jnp.bfloat16), 'guide', split_axis=0, concat...  24.5 us
    slice x1, local copies, waits for them, and re-layouts, masked_scores(): key_rows = page_rows[:, :, :half_width].reshape(count, span, KVH, HD)  16.9 us
    reduce_scatter x1, waiting for transfers between devices, body(): lax.psum_scatter(jnp.einsum('grc,cd->grd', selected, w_out, preferred_ele...  15 us
    gather x4, local copies, waits for them, and re-layouts, body(): pages_sent = pool[tables[held_request, :MIGP]]  11.9 us
    gather x1, local copies, waits for them, and re-layouts, gather_pages(): picked = pool[tables]  11.3 us
    ppermute x4, starting transfers between devices, shifted(): return lax.ppermute(value, axis, pairs)  8.66 us
  transfers between devices with their start and end apart: 9, of which 3 were waited for; matrix products, arithmetic and copies ran while one was open for 18% of the time, Pallas kernels for 0%

commit v1 on v0

--- a/solution.py
+++ b/solution.py
@@ -164,7 +164,15 @@
     )
     final = rms_scale(state_after, final_gain).astype(jnp.bfloat16)
     logits = jnp.dot(
-        lax.all_gather(final, "req", axis=0, tiled=True),
+        jnp.concatenate(
+            lax.all_to_all(
+                jnp.stack(lax.axis_size("req") * [final], 0),
+                axis_name="req",
+                split_axis=0,
+                concat_axis=0,
+            ),
+            0,
+        ),
         w_vocab,
         preferred_element_type=jnp.float32,
     )

time: 427 us -> 490 us (1.15)
  blocking collectives: 24.5 us -> 312 us
  waiting for transfers between devices: 246 us -> 20.2 us
  local copies, waits for them, and re-layouts: 77.8 us -> 83.9 us
    all_to_all x0 -> x1, blocking collectives: none -> 288 us  [body(): lax.all_to_all(jnp.stack(lax.axis_size('req') * [final], 0), axis_name='r...]
    all_gather x1 -> x0, waiting for transfers between devices: 226 us -> none  [body(): lax.all_gather(final, 'req', axis=0, tiled=True)]
    another operation x0 -> x1, local copies, waits for them, and re-layouts: none -> 6.17 us  [body(): jnp.stack(lax.axis_size('req') * [final], 0)]
    unnamed x17 -> x19, local copies, waits for them, and re-layouts: 32.1 us -> 32.1 us
  transfers between devices with their start and end apart: 9 -> 8, of which waited for: 3 -> 2; matrix products, arithmetic and copies ran while one was open for 18% -> 16% of each run, Pallas kernels for 0% -> 0%
where the time goes in v1:
time: 490 us; the launch traced here: 488 us
  blocking collectives  312 us (64%)
  local copies, waits for them, and re-layouts  83.9 us (17%)
  between operations  28.8 us (6%)
  waiting for transfers between devices  20.2 us (4%)
  matrix products  19 us (4%)
  starting transfers between devices  12.4 us (3%)
  other arithmetic  12.1 us (2%)
    all_to_all x1, blocking collectives, body(): lax.all_to_all(jnp.stack(lax.axis_size('req') * [final], 0), axis_name='r...  288 us
    unnamed x19, local copies, waits for them, and re-layouts  32.1 us
    all_to_all x1, blocking collectives, body(): lax.all_to_all(halves.astype(jnp.bfloat16), 'guide', split_axis=0, concat...  23.7 us
    slice x1, local copies, waits for them, and re-layouts, masked_scores(): key_rows = page_rows[:, :, :half_width].reshape(count, span, KVH, HD)  16.9 us
    reduce_scatter x1, waiting for transfers between devices, body(): lax.psum_scatter(jnp.einsum('grc,cd->grd', selected, w_out, preferred_ele...  15.3 us
    gather x4, local copies, waits for them, and re-layouts, body(): pages_sent = pool[tables[held_request, :MIGP]]  11.9 us
    gather x1, local copies, waits for them, and re-layouts, gather_pages(): picked = pool[tables]  11.3 us
  transfers between devices with their start and end apart: 8, of which 2 were waited for; matrix products, arithmetic and copies ran while one was open for 16% of the time, Pallas kernels for 0%

profile of v1, /device:TPU:32, one launch (start us, length us, event | category | flops | bytes accessed | tf_op | source)
XLA Modules:
  0.0 488.0 jit_solution(2344899492356520365)
XLA Ops:
  17.8 1.5 constant_dynamic-slice_fusion.8
  26.8 1.0 fusion.60
  27.9 2.6 gather_fusion
  30.5 1.9 collective-permute-start.1
  32.4 2.7 gather_fusion.1
  35.1 6.8 %collective-permute-start.2 = (bf16[2,64,640]{2,1,0:T(8,128)(2,1)S(1)}, bf16[2,64,640]{2,1,0:T(8,128)(2,1)S(1)}, u32[]{:S(2)}, u32[]{:S(2)}) collective-permute-start(bf16[2,64,640]{2,1,0:T(8,128)(2,1)S(1)} %gather_fusion.1), channel_id=1, source_target_pairs={{0,127},{1,0},{2,1},{3,2},{4,3},{5,4},{6,5},{7,6},{8,7},{9,8},{10,... | collective-permute-start | bytes 491528 | tf_op jit(solution)/shard_map/ppermute | solution.py:30
  41.9 3.3 gather_fusion.2
  45.2 3.3 gather_fusion.3
  48.5 1.0 fusion.21
  49.5 1.6 fusion.23
  51.1 2.7 collective-permute-start
  53.9 4.2 constant_dynamic-update-slice_fusion.4
  60.4 3.7 fusion
  65.8 1.6 constant_dynamic-update-slice_fusion.1
  67.4 1.6 constant_dynamic-update-slice_fusion
  69.0 11.3 %gather_fusion.4 = bf16[192,64,640]{2,1,0:T(8,128)(2,1)} fusion(bf16[54,64,640]{2,1,0:T(8,128)(2,1)} %constant_dynamic-update-slice_fusion, s32[1024]{0:T(1024)S(1)} %pad_clamp_fusion), kind=kCustom, calls=%fused_computation.4 | custom fusion | bytes 31458048 | tf_op jit(solution)/shard_map/gather | solution.py:69
  80.3 16.9 %fusion.71 = (bf16[24,512,320]{2,1,0:T(8,128)(2,1)}, bf16[24,512,320]{2,1,0:T(8,128)(2,1)}) fusion(bf16[24,512,640]{2,1,0:T(8,128)(2,1)} %bitcast.147), kind=kLoop, calls=%fused_computation.135 | loop fusion | bytes 31457280 | tf_op jit(solution)/shard_map/slice | solution.py:41
  97.2 11.6 %copy.27 = bf16[24,512,320]{1,2,0:T(8,128)(2,1)} copy(bf16[24,512,320]{2,1,0:T(8,128)(2,1)} %get-tuple-element.17) | data formatting | bytes 15728640
  108.7 11.5 %copy.28 = bf16[24,512,320]{1,2,0:T(8,128)(2,1)} copy(bf16[24,512,320]{2,1,0:T(8,128)(2,1)} %get-tuple-element.18) | data formatting | bytes 15728640
  120.2 0.9 convert_bitcast_fusion.2
  121.8 4.5 fusion.72
  127.9 5.8 %fusion.12 = bf16[24,5,4,64]{3,2,1,0:T(4,128)(2,1)S(1)} fusion(bf16[24,512,5,64]{1,3,2,0:T(8,128)(2,1)} %bitcast.150, f32[24,5,4,512]{3,2,1,0:T(4,128)} %copy-done.1, f32[24,5,4]{2,1,0:T(8,128)S(1)} %fusion.38, f32[24,5,4]{2,1,0:T(8,128)S(1)} %get-tuple-element.20, f32[24,5,64]{2,1,0:T(8,128)S(1)} %reshape.373, f32[24,5,4]{2,1,0:T(8,128)S(1)} %get-tuple-element.19), kind=kOutput, calls=%fused_computation.20 | convolution fusion | flops 32071680 | bytes 8945280 | tf_op jit(solution)/shard_map/rkgs,rskd->rkgd/dot_general | solution.py:57
  134.8 4.9 %collective-permute-done.5 = bf16[24,1280]{1,0:T(8,128)(2,1)S(1)} collective-permute-done((bf16[24,1280]{1,0:T(8,128)(2,1)S(1)}, bf16[24,1280]{1,0:T(8,128)(2,1)S(1)}, u32[]{:S(2)}, u32[]{:S(2)}) %collective-permute-start.5) | collective-permute-done | bytes 61472 | tf_op jit(solution)/shard_map/ppermute | solution.py:24
  139.7 1.2 fusion.4
  141.0 15.3 %reduce-scatter.5.cloned.1.call-done = bf16[1,24,2048]{2,1,0:T(8,128)(2,1)} async-done(((bf16[2,24,2048]{2,1,0:T(8,128)(2,1)}), bf16[1,24,2048]{2,1,0:T(8,128)(2,1)}) %reduce-scatter.5.cloned.1.call-update) | async-done | bytes 98320 | tf_op jit(solution)/shard_map/reduce_scatter | solution.py:156
  156.2 1.0 fusion.25
  157.3 1.0 fusion.36
  158.3 6.2 %stack.23 = bf16[128,24,2048]{2,1,0:T(8,128)(2,1)} broadcast(bf16[24,2048]{1,0:T(8,128)(2,1)S(1)} %fusion.36), dimensions={1,2} | broadcast | bytes 12681216 | tf_op jit(solution)/shard_map/stack | solution.py:169
  164.4 287.8 %all_to_all.10 = bf16[128,24,2048]{2,1,0:T(8,128)(2,1)S(1)} all-to-all(bf16[128,24,2048]{2,1,0:T(8,128)(2,1)} %stack.23), channel_id=1, replica_groups=mesh['guide'=2,'req'=128] {'req'}, dimensions={0} | all-to-all | bytes 25165824 | tf_op jit(solution)/shard_map/all_to_all | solution.py:168
  452.3 3.6 convolution_convert_fusion
  455.9 23.7 %all_to_all.11 = bf16[2,1536,250]{2,1,0:T(8,128)(2,1)S(1)} all-to-all(bf16[2,1536,250]{2,1,0:T(8,128)(2,1)S(1)} %convolution_convert_fusion), channel_id=1, replica_groups=mesh['guide'=2,'req'=128] {'guide'}, dimensions={0} | all-to-all | bytes 3072000 | tf_op jit(solution)/shard_map/all_to_all | solution.py:180
  479.8 1.3 fusion.9
  (65 shorter events, 11.1 us)
Async XLA Ops:
  6.5 133.2 %copy-start = (bf16[640,2048]{1,0:T(8,128)(2,1)S(1)}, bf16[640,2048]{1,0:T(8,128)(2,1)}, u32[]{:S(2)}) copy-start(bf16[640,2048]{1,0:T(8,128)(2,1)} %param.13) | copy-start | bytes 7864324
  6.5 113.7 %reduce-scatter.7.cloned.1.call-start = ((), (), s32[]{:S(2)}) async-start(), calls=%async_computation.5 | async-start | bytes 552960
  30.5 33.9 %collective-permute-start.1 = (bf16[2,64,640]{2,1,0:T(8,128)(2,1)S(1)}, bf16[2,64,640]{2,1,0:T(8,128)(2,1)S(1)}, u32[]{:S(2)}, u32[]{:S(2)}) collective-permute-start(bf16[2,64,640]{2,1,0:T(8,128)(2,1)S(1)} %gather_fusion), channel_id=1, source_target_pairs={{0,126},{1,127},{2,0},{3,1},{4,2},{5,3},{6,4},{7,5},{8,6},{9,7},{1... | collective-permute-start | bytes 491528 | tf_op jit(solution)/shard_map/ppermute | solution.py:30
  32.4 25.7 %copy-start.2 = (bf16[1,24,2048]{2,1,0:T(8,128)(2,1)S(1)}, bf16[1,24,2048]{2,1,0:T(8,128)(2,1)}, u32[]{:S(2)}) copy-start(bf16[1,24,2048]{2,1,0:T(8,128)(2,1)} %param.10) | copy-start | bytes 294916
  32.4 25.7 %copy-start.3 = (f32[2048]{0:T(1024)S(1)}, f32[2048]{0:T(1024)}, u32[]{:S(2)}) copy-start(f32[2048]{0:T(1024)} %param.11) | copy-start | bytes 24580
  35.1 30.0 %collective-permute-start.2 = (bf16[2,64,640]{2,1,0:T(8,128)(2,1)S(1)}, bf16[2,64,640]{2,1,0:T(8,128)(2,1)S(1)}, u32[]{:S(2)}, u32[]{:S(2)}) collective-permute-start(bf16[2,64,640]{2,1,0:T(8,128)(2,1)S(1)} %gather_fusion.1), channel_id=1, source_target_pairs={{0,127},{1,0},{2,1},{3,2},{4,3},{5,4},{6,5},{7,6},{8,7},{9,8},{10,... | collective-permute-start | bytes 491528 | tf_op jit(solution)/shard_map/ppermute | solution.py:30
  45.2 20.6 %collective-permute-start.3 = (bf16[2,64,640]{2,1,0:T(8,128)(2,1)}, bf16[2,64,640]{2,1,0:T(8,128)(2,1)}, u32[]{:S(2)}, u32[]{:S(2)}) collective-permute-start(bf16[2,64,640]{2,1,0:T(8,128)(2,1)} %gather_fusion.2), channel_id=1, source_target_pairs={{0,1},{1,2},{2,3},{3,4},{4,5},{5,6},{6,7},{7,8},{8,9},{9,10},{10,1... | collective-permute-start | bytes 491528 | tf_op jit(solution)/shard_map/ppermute | solution.py:30
  48.5 18.9 %collective-permute-start.4 = (bf16[2,64,640]{2,1,0:T(8,128)(2,1)}, bf16[2,64,640]{2,1,0:T(8,128)(2,1)}, u32[]{:S(2)}, u32[]{:S(2)}) collective-permute-start(bf16[2,64,640]{2,1,0:T(8,128)(2,1)} %gather_fusion.3), channel_id=1, source_target_pairs={{0,2},{1,3},{2,4},{3,5},{4,6},{5,7},{6,8},{7,9},{8,10},{9,11},{10,... | collective-permute-start | bytes 491528 | tf_op jit(solution)/shard_map/ppermute | solution.py:30
  51.1 9.3 %collective-permute-start = (bf16[24,2048]{1,0:T(8,128)(2,1)}, bf16[24,2048]{1,0:T(8,128)(2,1)}, u32[]{:S(2)}, u32[]{:S(2)}) collective-permute-start(bf16[24,2048]{1,0:T(8,128)(2,1)} %fusion.23), channel_id=1, source_target_pairs={{0,128},{128,0},{1,129},{129,1},{2,130},{130,2},{3,131},{131,3},{4... | collective-permute-start | bytes 294920 | tf_op jit(solution)/shard_map/ppermute | solution.py:24
  64.1 92.1 %reduce-scatter.5.cloned.1.call-start = ((), (), s32[]{:S(2)}) async-start(), calls=%async_computation.4 | async-start | bytes 294912 | tf_op jit(solution)/shard_map/reduce_scatter | solution.py:156
  126.2 0.9 copy-start.1
  133.7 23.5 %copy-start.4 = (f32[2048]{0:T(1024)S(1)}, f32[2048]{0:T(1024)}, u32[]{:S(2)}) copy-start(f32[2048]{0:T(1024)} %param.14) | copy-start | bytes 24580
  133.9 5.8 %collective-permute-start.5 = (bf16[24,1280]{1,0:T(8,128)(2,1)S(1)}, bf16[24,1280]{1,0:T(8,128)(2,1)S(1)}, u32[]{:S(2)}, u32[]{:S(2)}) collective-permute-start(bf16[24,1280]{1,0:T(8,128)(2,1)S(1)} %convert_element_type.87), channel_id=1, source_target_pairs={{0,128},{128,0},{1,129},{129,1},{2,130},{130,2},{3,131},{131,3},{4... | collective-permute-start | bytes 184328 | tf_op jit(solution)/shard_map/ppermute | solution.py:24
  164.4 287.9 %copy-start.5 = (bf16[2048,250]{1,0:T(8,128)(2,1)S(1)}, bf16[2048,250]{1,0:T(8,128)(2,1)}, u32[]{:S(2)}) copy-start(bf16[2048,250]{1,0:T(8,128)(2,1)} %param.15) | copy-start | bytes 3072004
Sparse Core Ops, SparseCore 0:
  64.3 17.4 reduce-scatter.6
  141.1 15.0 reduce-scatter.4
